TPU v7x, 32 devices: a whole 2x2x4 slice. The times are simulated.
32 devices in a mesh: blk: 4 (over x, core), st: 8 (over z, y).
Axes of the slice: x: 2, y: 2, z: 4, core: 2. Of those that a mesh axis runs over, the one named last changes fastest.
Arguments:
- voltages: bfloat16 [2, 4, 512, 34176], P(None, 'blk', 'st'), may hold values from -6 to 6
- filter_coeffs: float32 [12, 128], replicated, may hold values from -1.75 to 1.75
- station_gain: float32 [512], P('st'), may hold values from 0.5 to 5
- flags: int32 [4, 512], P('blk', 'st'), may hold values 0 or 1
- steer_index: int32 [512, 128], replicated, may hold values from 0 to 4095
Outputs:
- beams: bfloat16 [2, 128, 4, 256, 128], P(None, 'st', 'blk')
All inputs are finite; a program needn't handle non-finite values. No bound on the sum of `flags` on one device may be relied on, other than what follows from the above.
Results may differ from a plain program's by a relative error of at most 0.0074.
Values may be sent and summed in bfloat16 or wider, within the bound.
No kernel may reach another device: no remote copies, remote signals or barrier semaphores. Data moves between devices by JAX's collectives and lax.ppermute only.
A program may use at most 320 MiB of HBM per device.

v0:
```python
import math

import jax
import jax.numpy as jnp
from jax import lax
from jax.sharding import PartitionSpec as P

PHASES = 4096
AXES = ("blk", "st")


def dft_tables(width):
    counter = jnp.arange(width, dtype=jnp.int32)
    product = counter[:, None] * counter[None, :] % width
    angle = product.astype(jnp.float32) * (2.0 * math.pi / width)
    factor = 1.0 / math.sqrt(width)
    return (
        (jnp.cos(angle) * factor).astype(jnp.bfloat16),
        (jnp.sin(angle) * factor).astype(jnp.bfloat16),
    )


def polyphase(samples, filter_coeffs, row_gain):
    ntaps = filter_coeffs.shape[0]
    width = filter_coeffs.shape[1]
    grid = samples.astype(jnp.float32).reshape(2, samples.shape[1], -1, width)
    count = grid.shape[2] - ntaps + 1
    filtered = filter_coeffs[0][None, None, None, :] * grid[:, :, 0:count, :]
    for tap_no in range(1, ntaps):
        filtered = (
            filtered
            + filter_coeffs[tap_no][None, None, None, :] * grid[:, :, tap_no : tap_no + count, :]
        )
    return (filtered * row_gain[None, :, None, None]).astype(jnp.bfloat16)


def polyphase_flat(samples, filter_coeffs, row_gain):
    ntaps = filter_coeffs.shape[0]
    width = filter_coeffs.shape[1]
    count = samples.shape[2] // width - ntaps + 1
    span = count * width
    coeffs = jnp.tile(filter_coeffs, (1, count))
    filtered = coeffs[0][None, None, :] * samples[:, :, 0:span].astype(jnp.float32)
    for tap_no in range(1, ntaps):
        window = samples[:, :, tap_no * width : tap_no * width + span].astype(jnp.float32)
        filtered = filtered + coeffs[tap_no][None, None, :] * window
    filtered = (filtered * row_gain[None, :, None]).astype(jnp.bfloat16)
    return filtered.reshape(samples.shape[0], samples.shape[1], count, width)


def transform(filtered, cos_table, sin_table):
    flat_re = filtered[0]
    flat_im = filtered[1]
    dot = lambda a, b: jnp.einsum("stc,ck->stk", a, b, preferred_element_type=jnp.float32)
    out_re = dot(flat_re, cos_table) + dot(flat_im, sin_table)
    out_im = dot(flat_im, cos_table) - dot(flat_re, sin_table)
    return jnp.stack([out_re, out_im]).astype(jnp.bfloat16)


def batched(matrix, vectors):
    return jnp.einsum("ksu,kub->ksb", matrix, vectors, precision=lax.Precision.HIGHEST)


def iterate(rows_re, rows_im, steer_re, steer_im, diag_total, load):
    weight_re = steer_re / diag_total
    weight_im = steer_im / diag_total
    for sweep_no in range(2):
        prod_re = batched(rows_re, weight_re) - batched(rows_im, weight_im)
        prod_im = batched(rows_re, weight_im) + batched(rows_im, weight_re)
        next_re = weight_re + 0.5 * (steer_re - prod_re - load * weight_re) / diag_total
        next_im = weight_im + 0.5 * (steer_im - prod_im - load * weight_im) / diag_total
        weight_re, weight_im = (next_re, next_im)
    return weight_re, weight_im


def local(voltages, filter_coeffs, station_gain, flags, steer_index):
    nblk = lax.axis_size("blk")
    nst = lax.axis_size("st")
    ndev = nblk * nst
    ntaps, nk = filter_coeffs.shape
    cos_table, sin_table = dft_tables(nk)
    row_gain = station_gain * flags[0].astype(jnp.float32)
    samples = voltages[:, 0]
    ls = samples.shape[1]
    nt = samples.shape[2] // nk - ntaps + 1
    kc = nk // ndev
    stations = nst * ls
    counted = nblk * nt
    ngr = 4 if ls % 64 == 0 else 1
    gs = ls // ngr
    me = lax.axis_index("blk") * nst + lax.axis_index("st")
    eye = jnp.eye(stations, dtype=jnp.float32)
    factor = 1.0 / math.sqrt(stations)
    arrived = []
    later = []
    for g in range(ngr):
        part = samples[:, g * gs : (g + 1) * gs]
        filtered = polyphase_flat(part, filter_coeffs, row_gain[g * gs : (g + 1) * gs])
        local_spec = transform(filtered, cos_table, sin_table)
        send = local_spec.reshape(2, gs, nt, ndev, kc).transpose(3, 4, 0, 1, 2)
        if g == 0:
            arrived.append(lax.all_to_all(send, AXES, split_axis=0, concat_axis=0, tiled=True))
        else:
            later.append(send)
    if later:
        later, arrived = lax.optimization_barrier((later, arrived))
    lag = 2
    carries = bool(later) and kc > lag and steer_index.shape[1] // nst == gs

    def channel_send(c, beams_of):
        parts = [part[:, c] for part in later]
        if beams_of is not None:
            parts.append(beams_of)
        return lax.all_to_all(jnp.stack(parts, axis=1), AXES, split_axis=0, concat_axis=0, tiled=True)

    last = {}
    for c in range(min(lag, kc) if carries else kc):
        if later:
            last[c] = channel_send(c, None)
    hi = lax.Precision.HIGHEST
    got = {}
    prev = None
    outs = []
    for c in range(kc):
        pieces = [part[:, c] for part in arrived] + [last[c][:, i] for i in range(len(later))]
        if prev is not None:
            pieces, _ = lax.optimization_barrier((pieces, prev))
        if carries and c >= lag:
            got[c - lag] = last[c][:, len(later)]
        recv = jnp.stack(pieces, axis=2).reshape(nblk, nst, 2, ngr, gs, nt)
        spec = recv.transpose(2, 1, 3, 4, 0, 5).reshape(2 * stations, counted)
        gram = jnp.dot(spec, spec.T, preferred_element_type=jnp.float32)
        g00 = gram[:stations, :stations]
        g01 = gram[:stations, stations:]
        g10 = gram[stations:, :stations]
        g11 = gram[stations:, stations:]
        rows_re = (g00 + g11) / counted
        rows_im = (g10 - g01) / counted
        rows = jnp.concatenate([rows_re, rows_im], axis=0)
        diag_part = jnp.sum(rows_re * eye, axis=1)
        load = jnp.sum(diag_part) / stations + 1e-05
        channel_no = me * kc + c
        phase_int = steer_index * (channel_no + 1) % PHASES
        angle = phase_int.astype(jnp.float32) * (2.0 * math.pi / PHASES)
        steer_re = jnp.cos(angle)
        steer_im = jnp.sin(angle)
        diag_total = (diag_part + load)[:, None]
        weight_re = steer_re / diag_total
        weight_im = steer_im / diag_total
        nb = weight_re.shape[1]
        for sweep_no in range(2):
            both = jnp.concatenate([weight_re, weight_im], axis=1)
            prod = jnp.dot(rows, both, precision=hi)
            prod_re = prod[:stations, :nb] - prod[stations:, nb:]
            prod_im = prod[:stations, nb:] + prod[stations:, :nb]
            next_re = weight_re + 0.5 * (steer_re - prod_re - load * weight_re) / diag_total
            next_im = weight_im + 0.5 * (steer_im - prod_im - load * weight_im) / diag_total
            weight_re, weight_im = (next_re, next_im)
        half_re = weight_re.astype(jnp.bfloat16)
        half_im = weight_im.astype(jnp.bfloat16)
        lhs = jnp.concatenate(
            [jnp.concatenate([half_re, -half_im], axis=1), jnp.concatenate([half_im, half_re], axis=1)],
            axis=0,
        )
        beam = jnp.dot(lhs.T, spec, preferred_element_type=jnp.float32)
        beam = (beam * factor).astype(jnp.bfloat16)
        bc = nb // nst
        out = beam.reshape(2, nst, bc, nblk, nt).transpose(3, 1, 0, 2, 4).reshape(ndev, 2, bc, nt)
        prev = out
        outs.append(out)
        if carries and c + lag < kc:
            last[c + lag] = channel_send(c + lag, out)
    rest = [c for c in range(kc) if c not in got]
    sent = lax.all_to_all(jnp.stack([outs[c] for c in rest], axis=1), AXES, split_axis=0, concat_axis=0, tiled=True)
    for i, c in enumerate(rest):
        got[c] = sent[:, i]
    res = jnp.stack([got[c] for c in range(kc)], axis=4).transpose(1, 2, 3, 0, 4).reshape(2, bc, nt, ndev * kc)
    return res[:, :, None]


def fb_transform(filtered, cos_table, sin_table):
    width = cos_table.shape[0]
    flat_re = filtered[0].reshape(-1, width)
    flat_im = filtered[1].reshape(-1, width)
    out_re = jnp.dot(flat_re, cos_table, preferred_element_type=jnp.float32) + jnp.dot(
        flat_im, sin_table, preferred_element_type=jnp.float32
    )
    out_im = jnp.dot(flat_im, cos_table, preferred_element_type=jnp.float32) - jnp.dot(
        flat_re, sin_table, preferred_element_type=jnp.float32
    )
    return jnp.stack([out_re, out_im]).astype(jnp.bfloat16).reshape(filtered.shape)


def fb_batched(matrix, vectors):
    return jnp.einsum("ksu,kub->ksb", matrix, vectors, precision=lax.Precision.HIGHEST)


def fb_iterate(rows_re, rows_im, steer_re, steer_im, diag_total, load, collect, combine):
    weight_re = steer_re / diag_total
    weight_im = steer_im / diag_total
    for sweep_no in range(2):
        full_re, full_im = collect(weight_re, weight_im)
        prod_re = fb_batched(rows_re, full_re) - fb_batched(rows_im, full_im)
        prod_im = fb_batched(rows_re, full_im) + fb_batched(rows_im, full_re)
        prod_re, prod_im = combine(prod_re, prod_im)
        next_re = weight_re + 0.5 * (steer_re - prod_re - load * weight_re) / diag_total
        next_im = weight_im + 0.5 * (steer_im - prod_im - load * weight_im) / diag_total
        weight_re, weight_im = (next_re, next_im)
    return collect(weight_re, weight_im)


def unchanged(part_re, part_im):
    return (part_re, part_im)


def fb_local(voltages, filter_coeffs, station_gain, flags, steer_index):
    cos_table, sin_table = dft_tables(filter_coeffs.shape[1])
    row_gain = station_gain * flags[0].astype(jnp.float32)
    filtered = polyphase(voltages[:, 0], filter_coeffs, row_gain)
    local_spec = fb_transform(filtered, cos_table, sin_table)
    spectra = lax.all_to_all(local_spec, "st", split_axis=3, concat_axis=1, tiled=True)
    stations = spectra.shape[1]
    chans = spectra.shape[3]
    counted = lax.axis_size("blk") * spectra.shape[2]
    spec_re = spectra[0]
    spec_im = spectra[1]
    cov_re = jnp.einsum(
        "stk,utk->ksu", spec_re, spec_re, preferred_element_type=jnp.float32
    ) + jnp.einsum("stk,utk->ksu", spec_im, spec_im, preferred_element_type=jnp.float32)
    cov_im = jnp.einsum(
        "stk,utk->ksu", spec_im, spec_re, preferred_element_type=jnp.float32
    ) - jnp.einsum("stk,utk->ksu", spec_re, spec_im, preferred_element_type=jnp.float32)
    channel_ids = lax.axis_index("st") * chans + jnp.arange(chans, dtype=jnp.int32)
    total_re, total_im = lax.psum((cov_re, cov_im), "blk")
    rows_re = total_re / counted
    rows_im = total_im / counted
    diag_part = jnp.diagonal(rows_re, axis1=1, axis2=2)
    load = jnp.sum(diag_part, axis=1) / stations + 1e-05
    phase_int = steer_index[None, :, :] * (channel_ids + 1)[:, None, None] % PHASES
    angle = phase_int.astype(jnp.float32) * (2.0 * math.pi / PHASES)
    steer_re = jnp.cos(angle)
    steer_im = jnp.sin(angle)
    load_full = load[:, None, None]
    diag_total = (diag_part + load[:, None])[:, :, None]
    weight_re, weight_im = fb_iterate(
        rows_re, rows_im, steer_re, steer_im, diag_total, load_full, unchanged, unchanged
    )
    half_re = weight_re.astype(jnp.bfloat16)
    half_im = weight_im.astype(jnp.bfloat16)
    beam_re = jnp.einsum(
        "ksb,stk->btk", half_re, spec_re, preferred_element_type=jnp.float32
    ) + jnp.einsum("ksb,stk->btk", half_im, spec_im, preferred_element_type=jnp.float32)
    beam_im = jnp.einsum(
        "ksb,stk->btk", half_re, spec_im, preferred_element_type=jnp.float32
    ) - jnp.einsum("ksb,stk->btk", half_im, spec_re, preferred_element_type=jnp.float32)
    factor = 1.0 / math.sqrt(stations)
    beam_local = (jnp.stack([beam_re, beam_im]) * factor).astype(jnp.bfloat16)
    owned = lax.all_to_all(beam_local, "st", split_axis=1, concat_axis=3, tiled=True)
    return owned[:, :, None]


def body(voltages, filter_coeffs, station_gain, flags, steer_index):
    ndev = lax.axis_size("blk") * lax.axis_size("st")
    plan = local if filter_coeffs.shape[1] % ndev == 0 else fb_local
    return plan(voltages, filter_coeffs, station_gain, flags, steer_index)


def solution(mesh):
    return jax.shard_map(
        body,
        mesh=mesh,
        in_specs=(P(None, "blk", "st", None), P(), P("st"), P("blk", "st"), P()),
        out_specs=P(None, "st", "blk", None, None),
        check_vma=False,
    )
```

profile of v0, /device:TPU:0, one launch (start us, length us, event | category | flops | bytes accessed | tf_op | source)
XLA Modules:
  0.0 381.2 jit_solution(12013296360478522135)
XLA Ops:
  1.9 13.1 %multiply_convert_fusion = bf16[2,16,32768]{2,1,0:T(8,128)(2,1)S(1)} fusion(bf16[2,64,34176]{2,1,0:T(8,128)(2,1)} %bitcast.250, f32[16]{0:T(128)S(1)} %get-tuple-element.136, f32[32768]{0:T(1024)S(1)} %get-tuple-element.140, f32[32768]{0:T(1024)S(1)} %get-tuple-element.141, f32[32768]{0:T(1024)S(1)} %get-tuple-element.142, f32[32768]{0:T(1024)S(1)} %get-tuple-element.143, ...), kind=kLoop, calls=%fused_computation | loop fusion | flops 38797312 | bytes 28835904 | tf_op jit(solution)/shard_map/convert_element_type | solution.py:47
  21.0 7.7 %all-to-all-start = ((bf16[32,4,2,16,256]{4,3,2,1,0:T(8,128)(2,1)}), bf16[32,4,2,16,256]{4,3,2,1,0:T(8,128)(2,1)}, u32[]{:S(2)}, u32[]{:S(2)}) async-start(bf16[32,4,2,16,256]{4,3,2,1,0:T(8,128)(2,1)} %maximum_bitcast_fusion.3), calls=%async_computation | async-start | bytes 4194304 | tf_op jit(solution)/shard_map/all_to_all | solution.py:102
  28.7 13.5 %multiply_convert_fusion.3 = bf16[2,16,32768]{2,1,0:T(8,128)(2,1)S(1)} fusion(bf16[2,64,34176]{2,1,0:T(8,128)(2,1)} %bitcast.251, f32[16]{0:T(128)S(1)} %get-tuple-element.139, f32[32768]{0:T(1024)S(1)} %get-tuple-element.140, f32[32768]{0:T(1024)S(1)} %get-tuple-element.141, f32[32768]{0:T(1024)S(1)} %get-tuple-element.142, ...), kind=kLoop, calls=%fused_computation.3 | loop fusion | flops 38797312 | bytes 28835904 | tf_op jit(solution)/shard_map/convert_element_type | solution.py:47
  43.4 6.7 %multiply_convert_fusion.2 = bf16[2,16,32768]{2,1,0:T(8,128)(2,1)} fusion(bf16[2,64,34176]{2,1,0:T(8,128)(2,1)S(1)} %bitcast.254, f32[16]{0:T(128)S(1)} %get-tuple-element.138, f32[32768]{0:T(1024)S(1)} %get-tuple-element.140, f32[32768]{0:T(1024)S(1)} %get-tuple-element.141, f32[32768]{0:T(1024)S(1)} %get-tuple-element.142, ...), kind=kLoop, calls=%fused_computation.2 | loop fusion | flops 38797312 | bytes 28835904 | tf_op jit(solution)/shard_map/convert_element_type | solution.py:47
  50.2 6.7 %multiply_convert_fusion.1 = bf16[2,16,32768]{2,1,0:T(8,128)(2,1)} fusion(bf16[2,64,34176]{2,1,0:T(8,128)(2,1)S(1)} %bitcast.255, f32[16]{0:T(128)S(1)} %get-tuple-element.137, f32[32768]{0:T(1024)S(1)} %get-tuple-element.140, f32[32768]{0:T(1024)S(1)} %get-tuple-element.141, f32[32768]{0:T(1024)S(1)} %get-tuple-element.142, ...), kind=kLoop, calls=%fused_computation.1 | loop fusion | flops 38797312 | bytes 28835904 | tf_op jit(solution)/shard_map/convert_element_type | solution.py:47
  56.9 1.6 subtract_convert_fusion.3
  58.5 2.0 fusion.222
  63.5 1.6 add_convert_fusion.3
  69.3 1.7 subtract_convert_fusion.2
  72.4 1.6 copy.57
  74.7 1.7 add_convert_fusion.2
  76.3 2.0 stack.113
  81.1 1.6 subtract_convert_fusion.1
  93.2 2.9 fusion.330
  99.9 6.0 %all-to-all-start.1 = ((bf16[32,3,2,16,256]{4,3,2,1,0:T(8,128)(2,1)}), bf16[32,3,2,16,256]{4,3,2,1,0:T(8,128)(2,1)S(1)}, u32[]{:S(2)}, u32[]{:S(2)}) async-start(bf16[32,3,2,16,256]{4,3,2,1,0:T(8,128)(2,1)} %copy.64), calls=%async_computation.1 | async-start | bytes 3145728 | tf_op jit(solution)/shard_map/all_to_all | solution.py:114
  108.5 2.7 fusion.331
  111.2 33.6 %all-to-all-done.1 = bf16[32,3,2,16,256]{4,3,2,1,0:T(8,128)(2,1)S(1)} async-done(((bf16[32,3,2,16,256]{4,3,2,1,0:T(8,128)(2,1)}), bf16[32,3,2,16,256]{4,3,2,1,0:T(8,128)(2,1)S(1)}, u32[]{:S(2)}, u32[]{:S(2)}) %all-to-all-start.1) | async-done | bytes 1572896 | tf_op jit(solution)/shard_map/all_to_all | solution.py:114
  144.7 3.6 all-to-all-start.3
  148.7 2.7 copy.65
  152.0 2.4 fusion.334
  157.0 2.0 fusion.7
  160.5 2.0 fusion.6
  168.6 18.6 %all-to-all-done.3 = bf16[32,3,2,16,256]{4,3,2,1,0:T(8,128)(2,1)} async-done(((bf16[32,3,2,16,256]{4,3,2,1,0:T(8,128)(2,1)}), bf16[32,3,2,16,256]{4,3,2,1,0:T(8,128)(2,1)}, u32[]{:S(2)}, u32[]{:S(2)}) %all-to-all-start.3) | async-done | bytes 1572896 | tf_op jit(solution)/shard_map/all_to_all | solution.py:114
  187.2 3.1 all-to-all-start.2
  193.5 1.8 pad_maximum_fusion.2
  195.8 2.4 fusion.335
  198.1 2.1 fusion.26
  200.9 39.5 %all-to-all-done.2 = bf16[32,4,2,16,256]{4,3,2,1,0:T(8,128)(2,1)S(1)} async-done(((bf16[32,4,2,16,256]{4,3,2,1,0:T(8,128)(2,1)}), bf16[32,4,2,16,256]{4,3,2,1,0:T(8,128)(2,1)S(1)}, u32[]{:S(2)}, u32[]{:S(2)}) %all-to-all-start.2) | async-done | bytes 2097184 | tf_op jit(solution)/shard_map/all_to_all | solution.py:114
  243.1 1.8 pad_maximum_fusion.5
  245.3 2.4 fusion.336
  249.5 2.3 broadcast_divide_fusion.3
  251.8 2.0 fusion.3
  253.9 2.0 fusion.5
  256.0 3.2 fusion.130
  259.1 2.0 fusion.4
  264.5 1.6 pad_maximum_fusion.4
  267.6 3.8 %all-to-all-start.4 = ((bf16[32,4,2,16,256]{4,3,2,1,0:T(8,128)(2,1)}), bf16[32,4,2,16,256]{4,3,2,1,0:T(8,128)(2,1)}, u32[]{:S(2)}, u32[]{:S(2)}) async-start(bf16[32,4,2,16,256]{4,3,2,1,0:T(8,128)(2,1)} %copy.80), calls=%async_computation.4 | async-start | bytes 4194304 | tf_op jit(solution)/shard_map/all_to_all | solution.py:114
  271.5 3.0 fusion.2
  274.5 47.0 %all-to-all-done.4 = bf16[32,4,2,16,256]{4,3,2,1,0:T(8,128)(2,1)} async-done(((bf16[32,4,2,16,256]{4,3,2,1,0:T(8,128)(2,1)}), bf16[32,4,2,16,256]{4,3,2,1,0:T(8,128)(2,1)}, u32[]{:S(2)}, u32[]{:S(2)}) %all-to-all-start.4) | async-done | bytes 2097184 | tf_op jit(solution)/shard_map/all_to_all | solution.py:114
  321.5 2.5 slice_bitcast_fusion.18
  325.7 1.8 pad_maximum_fusion.7
  328.0 2.4 fusion.337
  333.2 2.0 fusion.1
  335.3 2.5 fusion.110
  337.9 2.0 fusion
  341.0 2.8 fusion.316
  347.4 29.7 %all_to_all.30 = bf16[32,2,2,16,256]{4,3,2,1,0:T(8,128)(2,1)S(1)} all-to-all(bf16[32,2,2,16,256]{4,3,2,1,0:T(8,128)(2,1)S(1)} %pad_maximum_fusion.19), channel_id=1, replica_groups=mesh['blk'=4,'st'=8] {'blk','st'}, dimensions={0} | all-to-all | bytes 2097152 | tf_op jit(solution)/shard_map/all_to_all | solution.py:174
  377.8 2.9 copy.102
  (184 shorter events, 70.1 us)
Async XLA Ops:
  21.0 22.4 %slice-start = ((s8[8749056]{0:T(1024)(128)(4,1)}), s8[360448]{0:T(1024)(128)(4,1)S(1)}, s32[]{:S(2)}) async-start(s8[8749056]{0:T(1024)(128)(4,1)} %bitcast.252), calls=%async_computation.6 | async-start | bytes 720896
  21.0 72.2 %all-to-all-start = ((bf16[32,4,2,16,256]{4,3,2,1,0:T(8,128)(2,1)}), bf16[32,4,2,16,256]{4,3,2,1,0:T(8,128)(2,1)}, u32[]{:S(2)}, u32[]{:S(2)}) async-start(bf16[32,4,2,16,256]{4,3,2,1,0:T(8,128)(2,1)} %maximum_bitcast_fusion.3), calls=%async_computation | async-start | bytes 4194304 | tf_op jit(solution)/shard_map/all_to_all | solution.py:102
  28.7 14.7 %slice-start.1 = ((s8[8749056]{0:T(1024)(128)(4,1)}), s8[4194304]{0:T(1024)(128)(4,1)S(1)}, s32[]{:S(2)}) async-start(s8[8749056]{0:T(1024)(128)(4,1)} %bitcast.252), calls=%async_computation.7 | async-start | bytes 8388608
  28.7 14.7 %slice-start.2 = ((s8[8749056]{0:T(1024)(128)(4,1)}), s8[4194304]{0:T(1024)(128)(4,1)S(1)}, s32[]{:S(2)}) async-start(s8[8749056]{0:T(1024)(128)(4,1)} %bitcast.252), calls=%async_computation.8 | async-start | bytes 8388608
  61.8 1.6 copy-start.2
  65.1 3.1 copy-start.4
  76.3 3.6 copy-start.3
  87.0 1.2 copy-start.6
  87.3 1.3 copy-start.7
  88.6 1.2 copy-start.8
  88.6 1.5 copy-start.9
  90.1 1.6 copy-start.10
  93.2 2.9 copy-start.1
  99.9 7.1 %copy-start.26 = (bf16[32,1,2,16,256]{4,3,2,0,1:T(8,128)(2,1)S(1)}, bf16[32,1,2,16,256]{4,3,2,0,1:T(8,128)(2,1)}, u32[]{:S(2)}) copy-start(bf16[32,1,2,16,256]{4,3,2,0,1:T(8,128)(2,1)} %get-tuple-element.70) | copy-start | bytes 1572868
  99.9 44.8 %all-to-all-start.1 = ((bf16[32,3,2,16,256]{4,3,2,1,0:T(8,128)(2,1)}), bf16[32,3,2,16,256]{4,3,2,1,0:T(8,128)(2,1)S(1)}, u32[]{:S(2)}, u32[]{:S(2)}) async-start(bf16[32,3,2,16,256]{4,3,2,1,0:T(8,128)(2,1)} %copy.64), calls=%async_computation.1 | async-start | bytes 3145728 | tf_op jit(solution)/shard_map/all_to_all | solution.py:114
  144.7 42.4 %all-to-all-start.3 = ((bf16[32,3,2,16,256]{4,3,2,1,0:T(8,128)(2,1)}), bf16[32,3,2,16,256]{4,3,2,1,0:T(8,128)(2,1)}, u32[]{:S(2)}, u32[]{:S(2)}) async-start(bf16[32,3,2,16,256]{4,3,2,1,0:T(8,128)(2,1)} %copy.71), calls=%async_computation.3 | async-start | bytes 3145728 | tf_op jit(solution)/shard_map/all_to_all | solution.py:114
  151.9 2.4 copy-start.21
  162.6 2.1 copy-start.22
  165.4 1.0 copy-start.28
  165.4 1.2 copy-start.29
  165.4 1.3 copy-start.30
  187.2 53.2 %all-to-all-start.2 = ((bf16[32,4,2,16,256]{4,3,2,1,0:T(8,128)(2,1)}), bf16[32,4,2,16,256]{4,3,2,1,0:T(8,128)(2,1)S(1)}, u32[]{:S(2)}, u32[]{:S(2)}) async-start(bf16[32,4,2,16,256]{4,3,2,1,0:T(8,128)(2,1)} %copy.67), calls=%async_computation.2 | async-start | bytes 4194304 | tf_op jit(solution)/shard_map/all_to_all | solution.py:114
  191.8 1.3 copy-start.25
  195.7 2.4 copy-start.17
  241.4 1.2 copy-start.24
  245.3 2.4 copy-start.15
  251.8 2.1 copy-start
  261.2 2.1 copy-start.18
  267.6 3.9 %copy-start.11 = (f32[512,128]{0,1:T(8,128)S(1)}, f32[512,128]{0,1:T(8,128)}, u32[]{:S(2)}) copy-start(f32[512,128]{0,1:T(8,128)} %get-tuple-element.100) | copy-start | bytes 786436
  267.6 3.9 %copy-start.13 = (f32[512,128]{0,1:T(8,128)S(1)}, f32[512,128]{0,1:T(8,128)}, u32[]{:S(2)}) copy-start(f32[512,128]{0,1:T(8,128)} %get-tuple-element.99) | copy-start | bytes 786436
  267.6 53.9 %all-to-all-start.4 = ((bf16[32,4,2,16,256]{4,3,2,1,0:T(8,128)(2,1)}), bf16[32,4,2,16,256]{4,3,2,1,0:T(8,128)(2,1)}, u32[]{:S(2)}, u32[]{:S(2)}) async-start(bf16[32,4,2,16,256]{4,3,2,1,0:T(8,128)(2,1)} %copy.80), calls=%async_computation.4 | async-start | bytes 4194304 | tf_op jit(solution)/shard_map/all_to_all | solution.py:114
  324.0 1.2 copy-start.23
  327.9 2.4 copy-start.19
  332.1 3.2 copy-start.5
  332.1 3.2 copy-start.12
  337.8 3.1 copy-start.14
  339.9 3.8 %copy-start.20 = (bf16[128,8,4,256]{3,1,2,0:T(8,128)(2,1)S(1)}, bf16[128,8,4,256]{3,1,2,0:T(8,128)(2,1)}, u32[]{:S(2)}) copy-start(bf16[128,8,4,256]{3,1,2,0:T(8,128)(2,1)} %copy-done.19) | copy-start | bytes 6291460
  343.8 1.2 copy-start.32
  343.8 1.2 copy-start.33
  344.5 1.6 copy-start.16
  347.4 29.8 %copy-start.27 = (bf16[32,2,16,256,1]{3,2,1,0,4:T(8,128)(2,1)S(1)}, bf16[32,2,16,256,1]{3,2,1,0,4:T(8,128)(2,1)}, u32[]{:S(2)}) copy-start(bf16[32,2,16,256,1]{3,2,1,0,4:T(8,128)(2,1)} %get-tuple-element.61) | copy-start | bytes 1572868
  347.4 29.8 %copy-start.31 = (bf16[32,2,16,256,1]{3,2,1,0,4:T(8,128)(2,1)S(1)}, bf16[32,2,16,256,1]{3,2,1,0,4:T(8,128)(2,1)}, u32[]{:S(2)}) copy-start(bf16[32,2,16,256,1]{3,2,1,0,4:T(8,128)(2,1)} %get-tuple-element.65) | copy-start | bytes 1572868
where the time goes:
time: 387 us; the launch traced here: 381 us
  waiting for transfers between devices  139 us (36%)
  other arithmetic  78.6 us (20%)
  local copies, waits for them, and re-layouts  59.4 us (15%)
  matrix products  46.4 us (12%)
  blocking collectives  29.7 us (8%)
  starting transfers between devices  24.2 us (6%)
  between operations  4.2 us (1%)
    all_to_all x4, waiting for transfers between devices, channel_send(): lax.all_to_all(jnp.stack(parts, axis=1), AXES, split_axis=0, concat_axis=...  139 us
    convert_element_type x4, other arithmetic, polyphase_flat(): filtered = (filtered * row_gain[None, :, None]).astype(jnp.bfloat16)  40.1 us
    all_to_all x1, blocking collectives, local(): lax.all_to_all(jnp.stack([outs[c] for c in rest], axis=1), AXES, split_ax...  29.7 us
    another operation x14, local copies, waits for them, and re-layouts, transform(): return jnp.stack([out_re, out_im]).astype(jnp.bfloat16)  17.5 us
    dot_general x8, matrix products, local(): prod = jnp.dot(rows, both, precision=hi)  17.3 us
    dot_general x16, matrix products, transform(): jnp.einsum('stc,ck->stk', a, b, preferred_element_type=jnp.float32)  16.7 us
    all_to_all x4, starting transfers between devices, channel_send(): lax.all_to_all(jnp.stack(parts, axis=1), AXES, split_axis=0, concat_axis=...  16.5 us
    dot_general x4, matrix products, local(): gram = jnp.dot(spec, spec.T, preferred_element_type=jnp.float32)  9.47 us
  transfers between devices with their start and end apart: 5, of which 4 were waited for; matrix products, arithmetic and copies ran while one was open for 26% of the time, Pallas kernels for 0%

commit v1 on v0

--- a/solution.py
+++ b/solution.py
@@ -105,12 +105,12 @@
     if later:
         later, arrived = lax.optimization_barrier((later, arrived))
     lag = 2
-    carries = bool(later) and kc > lag and steer_index.shape[1] // nst == gs
-
-    def channel_send(c, beams_of):
+    carries = bool(later) and kc > lag
+
+    def channel_send(c, after):
         parts = [part[:, c] for part in later]
-        if beams_of is not None:
-            parts.append(beams_of)
+        if after is not None:
+            parts, _ = lax.optimization_barrier((parts, after))
         return lax.all_to_all(jnp.stack(parts, axis=1), AXES, split_axis=0, concat_axis=0, tiled=True)
 
     last = {}
@@ -118,15 +118,12 @@
         if later:
             last[c] = channel_send(c, None)
     hi = lax.Precision.HIGHEST
-    got = {}
     prev = None
     outs = []
     for c in range(kc):
         pieces = [part[:, c] for part in arrived] + [last[c][:, i] for i in range(len(later))]
         if prev is not None:
             pieces, _ = lax.optimization_barrier((pieces, prev))
-        if carries and c >= lag:
-            got[c - lag] = last[c][:, len(later)]
         recv = jnp.stack(pieces, axis=2).reshape(nblk, nst, 2, ngr, gs, nt)
         spec = recv.transpose(2, 1, 3, 4, 0, 5).reshape(2 * stations, counted)
         gram = jnp.dot(spec, spec.T, preferred_element_type=jnp.float32)
@@ -170,11 +167,8 @@
         outs.append(out)
         if carries and c + lag < kc:
             last[c + lag] = channel_send(c + lag, out)
-    rest = [c for c in range(kc) if c not in got]
-    sent = lax.all_to_all(jnp.stack([outs[c] for c in rest], axis=1), AXES, split_axis=0, concat_axis=0, tiled=True)
-    for i, c in enumerate(rest):
-        got[c] = sent[:, i]
-    res = jnp.stack([got[c] for c in range(kc)], axis=4).transpose(1, 2, 3, 0, 4).reshape(2, bc, nt, ndev * kc)
+    sent = lax.all_to_all(jnp.stack(outs, axis=1), AXES, split_axis=0, concat_axis=0, tiled=True)
+    res = sent.transpose(2, 3, 4, 0, 1).reshape(2, bc, nt, ndev * kc)
     return res[:, :, None]
 
 

time: 387 us -> 392 us (1.013)
  blocking collectives: 29.7 us -> 52 us
  waiting for transfers between devices: 139 us -> 120 us
    all_to_all x1, blocking collectives: 29.7 us -> 52 us  [local(): lax.all_to_all(jnp.stack(outs, axis=1), AXES, split_axis=0, concat_axis=0...]
    all_to_all x4, waiting for transfers between devices: 139 us -> 120 us  [channel_send(): lax.all_to_all(jnp.stack(parts, axis=1), AXES, split_axis=0, concat_axis=...]
    slice x4 -> x0, local copies, waits for them, and re-layouts: 7.99 us -> none  [the longest x3 5.27 us: channel_send(): parts = [part[:, c] for part in later]]
    squeeze x0 -> x4, local copies, waits for them, and re-layouts: none -> 7.92 us  [the longest x3 5.18 us: channel_send(): parts = [part[:, c] for part in later]]
    unnamed x91 -> x75, local copies, waits for them, and re-layouts: 9.28 us -> 7.77 us
  transfers between devices with their start and end apart: 5 -> 5, of which waited for: 4 -> 4; matrix products, arithmetic and copies ran while one was open for 26% -> 25% of each run, Pallas kernels for 0% -> 0%
where the time goes in v1:
time: 392 us; the launch traced here: 386 us
  waiting for transfers between devices  120 us (31%)
  other arithmetic  78.1 us (20%)
  local copies, waits for them, and re-layouts  61.6 us (16%)
  blocking collectives  52 us (13%)
  matrix products  47 us (12%)
  starting transfers between devices  23.7 us (6%)
    all_to_all x4, waiting for transfers between devices, channel_send(): lax.all_to_all(jnp.stack(parts, axis=1), AXES, split_axis=0, concat_axis=...  120 us
    all_to_all x1, blocking collectives, local(): lax.all_to_all(jnp.stack(outs, axis=1), AXES, split_axis=0, concat_axis=0...  52 us
    convert_element_type x4, other arithmetic, polyphase_flat(): filtered = (filtered * row_gain[None, :, None]).astype(jnp.bfloat16)  40 us
    another operation x14, local copies, waits for them, and re-layouts, transform(): return jnp.stack([out_re, out_im]).astype(jnp.bfloat16)  20.7 us
    dot_general x8, matrix products, local(): prod = jnp.dot(rows, both, precision=hi)  17.6 us
    dot_general x16, matrix products, transform(): jnp.einsum('stc,ck->stk', a, b, preferred_element_type=jnp.float32)  16.3 us
    all_to_all x4, starting transfers between devices, channel_send(): lax.all_to_all(jnp.stack(parts, axis=1), AXES, split_axis=0, concat_axis=...  16 us
    dot_general x4, matrix products, local(): gram = jnp.dot(spec, spec.T, preferred_element_type=jnp.float32)  9.47 us
  transfers between devices with their start and end apart: 5, of which 4 were waited for; matrix products, arithmetic and copies ran while one was open for 25% of the time, Pallas kernels for 0%

profile of v1, /device:TPU:0, one launch (start us, length us, event | category | flops | bytes accessed | tf_op | source)
XLA Modules:
  0.0 386.0 jit_solution(3472205821944414054)
XLA Ops:
  1.9 13.1 %multiply_convert_fusion = bf16[2,16,32768]{2,1,0:T(8,128)(2,1)S(1)} fusion(bf16[2,64,34176]{2,1,0:T(8,128)(2,1)} %bitcast.247, f32[16]{0:T(128)S(1)} %get-tuple-element.142, f32[32768]{0:T(1024)S(1)} %get-tuple-element.146, f32[32768]{0:T(1024)S(1)} %get-tuple-element.147, f32[32768]{0:T(1024)S(1)} %get-tuple-element.148, f32[32768]{0:T(1024)S(1)} %get-tuple-element.149, ...), kind=kLoop, calls=%fused_computation | loop fusion | flops 38797312 | bytes 28835904 | tf_op jit(solution)/shard_map/convert_element_type | solution.py:47
  20.9 7.7 %all-to-all-start = ((bf16[32,4,2,16,256]{4,3,2,1,0:T(8,128)(2,1)}), bf16[32,4,2,16,256]{4,3,2,1,0:T(8,128)(2,1)}, u32[]{:S(2)}, u32[]{:S(2)}) async-start(bf16[32,4,2,16,256]{4,3,2,1,0:T(8,128)(2,1)} %maximum_bitcast_fusion.3), calls=%async_computation | async-start | bytes 4194304 | tf_op jit(solution)/shard_map/all_to_all | solution.py:102
  28.7 13.5 %multiply_convert_fusion.1 = bf16[2,16,32768]{2,1,0:T(8,128)(2,1)S(1)} fusion(bf16[2,64,34176]{2,1,0:T(8,128)(2,1)} %bitcast.248, f32[16]{0:T(128)S(1)} %get-tuple-element.143, f32[32768]{0:T(1024)S(1)} %get-tuple-element.146, f32[32768]{0:T(1024)S(1)} %get-tuple-element.147, f32[32768]{0:T(1024)S(1)} %get-tuple-element.148, ...), kind=kLoop, calls=%fused_computation.1 | loop fusion | flops 38797312 | bytes 28835904 | tf_op jit(solution)/shard_map/convert_element_type | solution.py:47
  43.4 6.7 %multiply_convert_fusion.2 = bf16[2,16,32768]{2,1,0:T(8,128)(2,1)} fusion(bf16[2,64,34176]{2,1,0:T(8,128)(2,1)S(1)} %bitcast.251, f32[16]{0:T(128)S(1)} %get-tuple-element.144, f32[32768]{0:T(1024)S(1)} %get-tuple-element.146, f32[32768]{0:T(1024)S(1)} %get-tuple-element.147, f32[32768]{0:T(1024)S(1)} %get-tuple-element.148, ...), kind=kLoop, calls=%fused_computation.2 | loop fusion | flops 38797312 | bytes 28835904 | tf_op jit(solution)/shard_map/convert_element_type | solution.py:47
  50.1 6.7 %multiply_convert_fusion.3 = bf16[2,16,32768]{2,1,0:T(8,128)(2,1)} fusion(bf16[2,64,34176]{2,1,0:T(8,128)(2,1)S(1)} %bitcast.252, f32[16]{0:T(128)S(1)} %get-tuple-element.145, f32[32768]{0:T(1024)S(1)} %get-tuple-element.146, f32[32768]{0:T(1024)S(1)} %get-tuple-element.147, f32[32768]{0:T(1024)S(1)} %get-tuple-element.148, ...), kind=kLoop, calls=%fused_computation.3 | loop fusion | flops 38797312 | bytes 28835904 | tf_op jit(solution)/shard_map/convert_element_type | solution.py:47
  56.8 1.6 add_convert_fusion.1
  59.0 2.2 stack.131
  61.3 2.8 copy.53
  64.0 1.7 subtract_convert_fusion.1
  67.2 1.6 copy.54
  70.0 1.6 add_convert_fusion.2
  75.2 1.6 subtract_convert_fusion.2
  76.8 2.0 stack.129
  81.6 1.6 add_convert_fusion.3
  84.5 1.6 copy.49
  86.8 1.6 subtract_convert_fusion.3
  94.5 2.8 slice_bitcast_fusion.23
  101.1 6.0 %all-to-all-start.1 = ((bf16[32,3,2,16,256]{4,3,2,1,0:T(8,128)(2,1)}), bf16[32,3,2,16,256]{4,3,2,1,0:T(8,128)(2,1)S(1)}, u32[]{:S(2)}, u32[]{:S(2)}) async-start(bf16[32,3,2,16,256]{4,3,2,1,0:T(8,128)(2,1)} %copy.58), calls=%async_computation.1 | async-start | bytes 3145728 | tf_op jit(solution)/shard_map/all_to_all | solution.py:114
  109.8 2.7 slice_bitcast_fusion.15
  112.5 33.4 %all-to-all-done.1 = bf16[32,3,2,16,256]{4,3,2,1,0:T(8,128)(2,1)S(1)} async-done(((bf16[32,3,2,16,256]{4,3,2,1,0:T(8,128)(2,1)}), bf16[32,3,2,16,256]{4,3,2,1,0:T(8,128)(2,1)S(1)}, u32[]{:S(2)}, u32[]{:S(2)}) %all-to-all-start.1) | async-done | bytes 1572896 | tf_op jit(solution)/shard_map/all_to_all | solution.py:114
  146.0 3.6 all-to-all-start.2
  150.9 2.7 copy.59
  154.1 2.4 fusion.330
  159.3 2.0 fusion.7
  162.8 2.0 fusion.6
  169.0 19.4 %all-to-all-done.2 = bf16[32,3,2,16,256]{4,3,2,1,0:T(8,128)(2,1)} async-done(((bf16[32,3,2,16,256]{4,3,2,1,0:T(8,128)(2,1)}), bf16[32,3,2,16,256]{4,3,2,1,0:T(8,128)(2,1)}, u32[]{:S(2)}, u32[]{:S(2)}) %all-to-all-start.2) | async-done | bytes 1572896 | tf_op jit(solution)/shard_map/all_to_all | solution.py:114
  191.5 1.8 pad_maximum_fusion.1
  193.8 2.4 fusion.331
  199.4 2.0 fusion.5
  202.7 2.0 fusion.4
  212.3 2.8 all-to-all-start.4
  217.8 36.2 %all-to-all-done.4 = bf16[32,3,2,16,256]{4,3,2,1,0:T(8,128)(2,1)S(1)} async-done(((bf16[32,3,2,16,256]{4,3,2,1,0:T(8,128)(2,1)}), bf16[32,3,2,16,256]{4,3,2,1,0:T(8,128)(2,1)S(1)}, u32[]{:S(2)}, u32[]{:S(2)}) %all-to-all-start.4) | async-done | bytes 1572896 | tf_op jit(solution)/shard_map/all_to_all | solution.py:114
  254.0 3.6 all-to-all-start.3
  259.4 1.8 pad_maximum_fusion.5
  261.7 2.4 fusion.333
  265.6 30.8 %all-to-all-done.3 = bf16[32,3,2,16,256]{4,3,2,1,0:T(8,128)(2,1)} async-done(((bf16[32,3,2,16,256]{4,3,2,1,0:T(8,128)(2,1)}), bf16[32,3,2,16,256]{4,3,2,1,0:T(8,128)(2,1)}, u32[]{:S(2)}, u32[]{:S(2)}) %all-to-all-start.3) | async-done | bytes 1572896 | tf_op jit(solution)/shard_map/all_to_all | solution.py:114
  299.6 1.8 pad_maximum_fusion.3
  301.9 2.4 fusion.332
  304.2 2.0 fusion.28
  308.2 3.3 fusion.3
  311.5 2.3 fusion.130
  313.8 2.0 fusion.2
  315.9 2.0 fusion.1
  317.9 2.3 fusion.110
  320.2 2.0 fusion
  322.3 2.4 fusion.316
  330.5 52.0 %all_to_all.30 = bf16[32,4,2,16,256]{4,3,2,1,0:T(8,128)(2,1)S(1)} all-to-all(bf16[32,4,2,16,256]{4,3,2,1,0:T(8,128)(2,1)S(1)} %copy.85), channel_id=1, replica_groups=mesh['blk'=4,'st'=8] {'blk','st'}, dimensions={0} | all-to-all | bytes 4194304 | tf_op jit(solution)/shard_map/all_to_all | solution.py:170
  382.8 2.9 copy.87
  (168 shorter events, 74.1 us)
Async XLA Ops:
  20.9 22.4 %slice-start = ((s8[8749056]{0:T(1024)(128)(4,1)}), s8[360448]{0:T(1024)(128)(4,1)S(1)}, s32[]{:S(2)}) async-start(s8[8749056]{0:T(1024)(128)(4,1)} %bitcast.249), calls=%async_computation.6 | async-start | bytes 720896
  20.9 73.6 %all-to-all-start = ((bf16[32,4,2,16,256]{4,3,2,1,0:T(8,128)(2,1)}), bf16[32,4,2,16,256]{4,3,2,1,0:T(8,128)(2,1)}, u32[]{:S(2)}, u32[]{:S(2)}) async-start(bf16[32,4,2,16,256]{4,3,2,1,0:T(8,128)(2,1)} %maximum_bitcast_fusion.3), calls=%async_computation | async-start | bytes 4194304 | tf_op jit(solution)/shard_map/all_to_all | solution.py:102
  28.6 14.7 %slice-start.1 = ((s8[8749056]{0:T(1024)(128)(4,1)}), s8[4194304]{0:T(1024)(128)(4,1)S(1)}, s32[]{:S(2)}) async-start(s8[8749056]{0:T(1024)(128)(4,1)} %bitcast.249), calls=%async_computation.7 | async-start | bytes 8388608
  28.7 14.7 %slice-start.2 = ((s8[8749056]{0:T(1024)(128)(4,1)}), s8[4194304]{0:T(1024)(128)(4,1)S(1)}, s32[]{:S(2)}) async-start(s8[8749056]{0:T(1024)(128)(4,1)} %bitcast.249), calls=%async_computation.8 | async-start | bytes 8388608
  65.7 3.1 copy-start.3
  76.8 3.6 copy-start.2
  88.4 2.1 copy-start.4
  88.4 2.1 copy-start.5
  90.5 1.5 copy-start.6
  90.5 2.3 copy-start.7
  92.8 1.5 copy-start.8
  94.5 2.8 copy-start.1
  101.1 6.0 %copy-start.25 = (s32[512,128]{1,0:T(8,128)S(1)}, s32[512,128]{1,0:T(8,128)}, u32[]{:S(2)}) copy-start(s32[512,128]{1,0:T(8,128)} %param.9) | copy-start | bytes 786436
  101.1 44.8 %all-to-all-start.1 = ((bf16[32,3,2,16,256]{4,3,2,1,0:T(8,128)(2,1)}), bf16[32,3,2,16,256]{4,3,2,1,0:T(8,128)(2,1)S(1)}, u32[]{:S(2)}, u32[]{:S(2)}) async-start(bf16[32,3,2,16,256]{4,3,2,1,0:T(8,128)(2,1)} %copy.58), calls=%async_computation.1 | async-start | bytes 3145728 | tf_op jit(solution)/shard_map/all_to_all | solution.py:114
  146.0 42.4 %all-to-all-start.2 = ((bf16[32,3,2,16,256]{4,3,2,1,0:T(8,128)(2,1)}), bf16[32,3,2,16,256]{4,3,2,1,0:T(8,128)(2,1)}, u32[]{:S(2)}, u32[]{:S(2)}) async-start(bf16[32,3,2,16,256]{4,3,2,1,0:T(8,128)(2,1)} %copy.63), calls=%async_computation.2 | async-start | bytes 3145728 | tf_op jit(solution)/shard_map/all_to_all | solution.py:114
  149.6 1.0 copy-start.24
  154.1 2.4 copy-start.13
  164.8 2.1 copy-start.14
  168.1 21.8 %copy-start.19 = (bf16[32,2,16,256]{3,2,1,0:T(8,128)(2,1)S(1)}, bf16[32,2,16,256]{3,2,1,0:T(8,128)(2,1)}, u32[]{:S(2)}) copy-start(bf16[32,2,16,256]{3,2,1,0:T(8,128)(2,1)} %get-tuple-element.31) | copy-start | bytes 1572868
  193.8 2.4 copy-start.15
  204.8 2.1 copy-start.16
  208.4 2.5 copy-start.21
  208.4 2.5 copy-start.22
  208.4 2.5 copy-start.23
  212.3 2.8 copy-start.20
  212.3 41.7 %all-to-all-start.4 = ((bf16[32,3,2,16,256]{4,3,2,1,0:T(8,128)(2,1)}), bf16[32,3,2,16,256]{4,3,2,1,0:T(8,128)(2,1)S(1)}, u32[]{:S(2)}, u32[]{:S(2)}) async-start(bf16[32,3,2,16,256]{4,3,2,1,0:T(8,128)(2,1)} %copy.79), calls=%async_computation.4 | async-start | bytes 3145728 | tf_op jit(solution)/shard_map/all_to_all | solution.py:114
  254.0 42.4 %all-to-all-start.3 = ((bf16[32,3,2,16,256]{4,3,2,1,0:T(8,128)(2,1)}), bf16[32,3,2,16,256]{4,3,2,1,0:T(8,128)(2,1)}, u32[]{:S(2)}, u32[]{:S(2)}) async-start(bf16[32,3,2,16,256]{4,3,2,1,0:T(8,128)(2,1)} %copy.71), calls=%async_computation.3 | async-start | bytes 3145728 | tf_op jit(solution)/shard_map/all_to_all | solution.py:114
  261.7 2.4 copy-start.9
  301.9 2.4 copy-start.11
  311.5 2.3 copy-start
  322.3 3.4 copy-start.12
  326.5 1.6 copy-start.10
  328.8 1.0 copy-start.17
  328.8 1.2 copy-start.18
